TPU v7x, 32 devices: a whole 2x2x4 slice. The times are simulated.
32 devices in a mesh: ctx: 8 (over z, y), tp: 4 (over x, core).
Axes of the slice: x: 2, y: 2, z: 4, core: 2. Of those that a mesh axis runs over, the one named last changes fastest.
Arguments:
- tokens: bfloat16 [1024, 4096], P('ctx'), may hold values from -6 to 6
- w_query: bfloat16 [4096, 2048], P('ctx', 'tp'), may hold values from -0.09375 to 0.09375
- w_key: bfloat16 [4096, 2048], P('ctx', 'tp'), may hold values from -0.09375 to 0.09375
- w_value: bfloat16 [4096, 2048], P('ctx', 'tp'), may hold values from -0.09375 to 0.09375
- taps_query: float32 [3, 2048], P(None, 'tp'), may hold values from -3.5 to 3.5
- taps_key: float32 [3, 2048], P(None, 'tp'), may hold values from -3.5 to 3.5
- taps_value: float32 [3, 2048], P(None, 'tp'), may hold values from -3.5 to 3.5
- decay_rate: float32 [16, 2048], P(None, 'tp'), may hold values from 1e-05 to 0.03
- residue: float32 [16, 2048], P(None, 'tp'), may hold values from -1.5 to 1.5
- skip_gain: float32 [2048], P('tp'), may hold values from -3 to 3
- w_out: bfloat16 [2048, 4096], P('ctx', 'tp'), may hold values from -0.125 to 0.125
Outputs:
- layer_out: bfloat16 [1024, 4096], P('ctx', 'tp')
All inputs are finite; a program needn't handle non-finite values.
Results may differ from a plain program's by a relative error of at most 0.015.
Values may be sent and summed in bfloat16 or wider, within the bound.
No kernel may reach another device: no remote copies, remote signals or barrier semaphores. Data moves between devices by JAX's collectives and lax.ppermute only.
A program may use at most 128 MiB of HBM per device.

v0:
```python
import jax
import jax.numpy as jnp
from jax import lax
from jax.sharding import PartitionSpec as P


def short_conv(padded, taps):
    return taps[0] * padded[2:] + taps[1] * padded[1:-1] + taps[2] * padded[:-2]


def modal_long_conv(signal, rates, residues, skips):
    length, width = signal.shape
    order = rates.shape[0]
    ctx_count = lax.axis_size("ctx")
    me = lax.axis_index("ctx")
    coefs = residues * jnp.sqrt(2.0 * rates)
    times = jnp.arange(length, dtype=jnp.float32)[:, None, None]
    grow = jnp.exp(rates[None] * times)
    decay = jnp.exp(-rates[None] * times)
    lifted = (grow * signal[:, None, :]).reshape(length, order * width)
    rows = jnp.arange(length, dtype=jnp.int32)
    lower = (rows[:, None] >= rows[None, :]).astype(jnp.float32)
    running = jnp.matmul(lower, lifted, precision=lax.Precision.HIGHEST).reshape(
        length, order, width
    )
    end_state = running[length - 1] * jnp.exp(-rates * (length - 1))
    states = lax.all_gather(end_state, "ctx", axis=0, tiled=False)
    chunk_ids = jnp.arange(ctx_count, dtype=jnp.int32)
    gap = jnp.maximum(me - 1 - chunk_ids, 0).astype(jnp.float32)
    carry_w = jnp.where(
        (chunk_ids < me)[:, None, None], jnp.exp(-rates[None] * (gap[:, None, None] * length)), 0.0
    )
    carried = jnp.sum(carry_w * states, axis=0) * jnp.exp(-rates)
    total = running + carried[None]
    mixed = jnp.sum(coefs[None] * decay * total, axis=1)
    return mixed + skips * signal


def body(
    tokens,
    w_query,
    w_key,
    w_value,
    taps_query,
    taps_key,
    taps_value,
    decay_rate,
    residue,
    skip_gain,
    w_out,
):
    ctx_count = lax.axis_size("ctx")
    halo = lax.ppermute(tokens[-2:], "ctx", perm=[(i, i + 1) for i in range(ctx_count - 1)])
    rows = jnp.concatenate([halo, tokens], axis=0)

    def project(piece):
        full = lax.all_gather(piece, "ctx", axis=0, tiled=True)
        out = jnp.dot(rows, full, preferred_element_type=jnp.float32)
        return out.astype(jnp.bfloat16).astype(jnp.float32)

    queries = project(w_query)
    keys_proj = project(w_key)
    values_proj = project(w_value)
    gate = short_conv(queries, taps_query).astype(jnp.bfloat16)
    product = (short_conv(keys_proj, taps_key) * short_conv(values_proj, taps_value)).astype(
        jnp.bfloat16
    )
    mixed = modal_long_conv(product.astype(jnp.float32), decay_rate, residue, skip_gain)
    mixed = mixed.astype(jnp.bfloat16)
    gated = (gate.astype(jnp.float32) * mixed.astype(jnp.float32)).astype(jnp.bfloat16)
    features = lax.all_gather(gated, "tp", axis=1, tiled=True)
    result = jnp.dot(
        features,
        lax.all_gather(w_out, "ctx", axis=0, tiled=True),
        preferred_element_type=jnp.float32,
    )
    return result.astype(jnp.bfloat16)


def solution(mesh):
    in_specs = (
        P("ctx", None),
        P("ctx", "tp"),
        P("ctx", "tp"),
        P("ctx", "tp"),
        P(None, "tp"),
        P(None, "tp"),
        P(None, "tp"),
        P(None, "tp"),
        P(None, "tp"),
        P("tp"),
        P("ctx", "tp"),
    )
    out_specs = P("ctx", "tp")
    return jax.shard_map(body, mesh=mesh, in_specs=in_specs, out_specs=out_specs, check_vma=False)
```

profile of v0, /device:TPU:0, one launch (start us, length us, event | category | flops | bytes accessed | tf_op | source)
XLA Modules:
  0.0 319.4 jit_solution(1594210370774384721)
XLA Ops:
  6.5 0.7 all-gather.10.cloned.1.call-update
  7.3 0.7 all-gather.8.cloned.1.call-update
  8.1 0.7 all-gather.6.cloned.1.call-update
  8.8 0.5 all-gather.12.cloned.1.call-update
  9.3 0.9 slice.62
  10.2 4.9 %collective-permute-start = (bf16[2,4096]{1,0:T(2,128)(2,1)S(1)}, bf16[2,4096]{1,0:T(2,128)(2,1)S(1)}, u32[]{:S(2)}, u32[]{:S(2)}) collective-permute-start(bf16[2,4096]{1,0:T(2,128)(2,1)S(1)} %slice.62), channel_id=1, source_target_pairs={{0,4},{4,8},{8,12},{12,16},{16,20},{20,24},{24,28},{1,5},{5,9},{9,... | collective-permute-start | bytes 49160 | tf_op jit(solution)/shard_map/ppermute | solution.py:53
  15.1 0.8 fusion.26
  15.9 0.8 fusion.25
  16.7 0.8 fusion.24
  17.5 0.8 copy.12
  18.3 67.3 %all-gather.10.cloned.1.call-done = bf16[4096,512]{1,0:T(8,128)(2,1)} async-done(((bf16[512,512]{1,0:T(8,128)(2,1)}), bf16[4096,512]{1,0:T(8,128)(2,1)}) %all-gather.10.cloned.1.call-update) | async-done | bytes 4194320 | tf_op jit(solution)/shard_map/all_gather | solution.py:57
  85.6 3.3 %fusion.8 = f32[130,512]{1,0:T(8,128)S(1)} fusion(bf16[4096,512]{1,0:T(8,128)(2,1)} %all-gather.10.cloned.1.call-done, bf16[128,4096]{1,0:T(8,128)(2,1)} %param.11, bf16[2,4096]{1,0:T(2,128)(2,1)S(1)} %collective-permute-done), kind=kOutput, calls=%fused_computation.11 | convolution fusion | flops 547522560 | bytes 5525504 | tf_op jit(solution)/shard_map/dot_general | solution.py:58
  88.9 70.5 %all-gather.8.cloned.1.call-done = bf16[4096,512]{1,0:T(8,128)(2,1)} async-done(((bf16[512,512]{1,0:T(8,128)(2,1)}), bf16[4096,512]{1,0:T(8,128)(2,1)}) %all-gather.8.cloned.1.call-update) | async-done | bytes 4194320 | tf_op jit(solution)/shard_map/all_gather | solution.py:57
  159.4 2.9 fusion.9
  163.1 3.4 %copy.13 = f32[16,8,16,512]{3,1,2,0:T(8,128)S(1)} copy(f32[16,8,16,512]{3,2,1,0:T(8,128)S(1)} %bitcast.28) | data formatting | bytes 8388608
  166.5 2.9 fusion.2
  169.5 5.2 %copy.14 = f32[16,8,16,512]{3,2,1,0:T(8,128)} copy(f32[16,8,16,512]{3,1,2,0:T(8,128)S(1)} %bitcast.26) | data formatting | bytes 8388608
  174.9 31.8 %all-gather = f32[128,512]{1,0:T(8,128)S(1)} all-gather(f32[16,512]{1,0:T(8,128)S(1)} %get-tuple-element.6), channel_id=2, replica_groups=mesh['ctx'=8,'tp'=4] {'ctx'}, dimensions={0}, use_global_device_ids=true | all-gather | bytes 294912 | tf_op jit(solution)/shard_map/all_gather | solution.py:27
  206.8 28.2 %all-gather.6.cloned.1.call-done = bf16[4096,512]{1,0:T(8,128)(2,1)} async-done(((bf16[512,512]{1,0:T(8,128)(2,1)}), bf16[4096,512]{1,0:T(8,128)(2,1)}) %all-gather.6.cloned.1.call-update) | async-done | bytes 4194320 | tf_op jit(solution)/shard_map/all_gather | solution.py:57
  235.0 3.1 fusion.10
  238.4 1.5 fusion.1
  240.1 7.2 %all_gather.26 = bf16[128,2048]{1,0:T(8,128)(2,1)S(1)} all-gather(bf16[128,512]{1,0:T(8,128)(2,1)S(1)} %multiply_convert_fusion), channel_id=1, replica_groups=mesh['ctx'=8,'tp'=4] {'tp'}, dimensions={1}, use_global_device_ids=true | all-gather | bytes 655360 | tf_op jit(solution)/shard_map/all_gather | solution.py:71
  247.2 62.0 %all-gather.12.cloned.1.call-done = bf16[2048,1024]{1,0:T(8,128)(2,1)} async-done(((bf16[256,1024]{1,0:T(8,128)(2,1)}), bf16[2048,1024]{1,0:T(8,128)(2,1)}) %all-gather.12.cloned.1.call-update) | async-done | bytes 4194320 | tf_op jit(solution)/shard_map/all_gather | solution.py:74
  309.2 3.6 %convolution_convert_fusion = bf16[128,1024]{1,0:T(8,128)(2,1)} fusion(bf16[128,2048]{1,0:T(8,128)(2,1)S(1)} %all_gather.26, bf16[2048,1024]{1,0:T(8,128)(2,1)} %all-gather.12.cloned.1.call-done), kind=kOutput, calls=%fused_computation.9 | convolution fusion | flops 537001984 | bytes 4980736 | tf_op jit(solution)/shard_map/dot_general | solution.py:72
  (25 shorter events, 1.6 us)
Async XLA Ops:
  6.5 152.9 %copy-start.4 = (bf16[128,4096]{1,0:T(8,128)(2,1)S(1)}, bf16[128,4096]{1,0:T(8,128)(2,1)}, u32[]{:S(2)}) copy-start(bf16[128,4096]{1,0:T(8,128)(2,1)} %param.11) | copy-start | bytes 3145732
  6.5 79.1 %all-gather.10.cloned.1.call-start = ((), (), s32[]{:S(2)}) async-start(), calls=%async_computation.2 | async-start | bytes 4718592 | tf_op jit(solution)/shard_map/all_gather | solution.py:57
  7.3 152.2 %all-gather.8.cloned.1.call-start = ((), (), s32[]{:S(2)}) async-start(), calls=%async_computation.1 | async-start | bytes 4718592 | tf_op jit(solution)/shard_map/all_gather | solution.py:57
  8.0 227.0 %all-gather.6.cloned.1.call-start = ((), (), s32[]{:S(2)}) async-start(), calls=%async_computation | async-start | bytes 4718592 | tf_op jit(solution)/shard_map/all_gather | solution.py:57
  8.7 300.5 %all-gather.12.cloned.1.call-start = ((), (), s32[]{:S(2)}) async-start(), calls=%async_computation.3 | async-start | bytes 4718592 | tf_op jit(solution)/shard_map/all_gather | solution.py:74
  10.2 8.1 %collective-permute-start = (bf16[2,4096]{1,0:T(2,128)(2,1)S(1)}, bf16[2,4096]{1,0:T(2,128)(2,1)S(1)}, u32[]{:S(2)}, u32[]{:S(2)}) collective-permute-start(bf16[2,4096]{1,0:T(2,128)(2,1)S(1)} %slice.62), channel_id=1, source_target_pairs={{0,4},{4,8},{8,12},{12,16},{16,20},{20,24},{24,28},{1,5},{5,9},{9,... | collective-permute-start | bytes 49160 | tf_op jit(solution)/shard_map/ppermute | solution.py:53
  169.4 5.4 %copy-start.1 = (f32[16,512]{1,0:T(8,128)S(1)}, f32[16,512]{1,0:T(8,128)}, u32[]{:S(2)}) copy-start(f32[16,512]{1,0:T(8,128)} %param.18) | copy-start | bytes 98308
  169.5 5.4 %copy-start.2 = (f32[16,512]{1,0:T(8,128)S(1)}, f32[16,512]{1,0:T(8,128)}, u32[]{:S(2)}) copy-start(f32[16,512]{1,0:T(8,128)} %param.19) | copy-start | bytes 98308
  206.8 33.1 %copy-start.3 = (f32[512]{0:T(512)S(1)}, f32[512]{0:T(512)}, u32[]{:S(2)}) copy-start(f32[512]{0:T(512)} %param.20) | copy-start | bytes 6148
  235.0 3.4 %copy-start = (f32[16,8,16,512]{3,2,1,0:T(8,128)S(1)}, f32[16,8,16,512]{3,2,1,0:T(8,128)}, u32[]{:S(2)}) copy-start(f32[16,8,16,512]{3,2,1,0:T(8,128)} %copy.14) | copy-start | bytes 12582916
Sparse Core Ops, SparseCore 0:
  9.5 76.0 all-gather.9
  87.7 71.6 all-gather.7
  161.6 73.3 all-gather.5
  237.0 72.2 all-gather.11
where the time goes:
time: 320 us; the launch traced here: 319 us
  waiting for transfers between devices  231 us (72%)
  blocking collectives  39 us (12%)
  matrix products  15.8 us (5%)
  local copies, waits for them, and re-layouts  13.7 us (4%)
  between operations  13.3 us (4%)
  starting transfers between devices  4.99 us (2%)
    all_gather x3, waiting for transfers between devices, project(): full = lax.all_gather(piece, 'ctx', axis=0, tiled=True)  166 us
    all_gather x1, waiting for transfers between devices, body(): lax.all_gather(w_out, 'ctx', axis=0, tiled=True)  62 us
    all_gather x1, blocking collectives, modal_long_conv(): states = lax.all_gather(end_state, 'ctx', axis=0, tiled=False)  31.8 us
    unnamed x13, local copies, waits for them, and re-layouts  9.79 us
    dot_general x3, matrix products, project(): out = jnp.dot(rows, full, preferred_element_type=jnp.float32)  9.3 us
    all_gather x1, blocking collectives, body(): features = lax.all_gather(gated, 'tp', axis=1, tiled=True)  7.19 us
  transfers between devices with their start and end apart: 5, of which 4 were waited for; matrix products, arithmetic and copies ran while one was open for 9% of the time, Pallas kernels for 0%

commit v1 on v0

--- a/solution.py
+++ b/solution.py
@@ -2,6 +2,17 @@
 import jax.numpy as jnp
 from jax import lax
 from jax.sharding import PartitionSpec as P
+
+
+def collect(value, axis, dim):
+    ways = lax.axis_size(axis)
+    pieces = [value]
+    for far in range(1, ways):
+        pieces.append(
+            lax.ppermute(pieces[far - 1], axis, [(d, (d - 1) % ways) for d in range(ways)])
+        )
+    line = jnp.concatenate(pieces, axis=dim)
+    return jnp.roll(line, lax.axis_index(axis) * value.shape[dim], axis=dim)
 
 
 def short_conv(padded, taps):
@@ -69,11 +80,7 @@
     mixed = mixed.astype(jnp.bfloat16)
     gated = (gate.astype(jnp.float32) * mixed.astype(jnp.float32)).astype(jnp.bfloat16)
     features = lax.all_gather(gated, "tp", axis=1, tiled=True)
-    result = jnp.dot(
-        features,
-        lax.all_gather(w_out, "ctx", axis=0, tiled=True),
-        preferred_element_type=jnp.float32,
-    )
+    result = jnp.dot(features, collect(w_out, "ctx", 0), preferred_element_type=jnp.float32)
     return result.astype(jnp.bfloat16)
 
 

time: 320 us -> 309 us (0.966)
  waiting for transfers between devices: 231 us -> 170 us
  starting transfers between devices: 4.99 us -> 38.6 us
  local copies, waits for them, and re-layouts: 13.7 us -> 30.3 us
    ppermute x0 -> x7, waiting for transfers between devices: none -> 110 us  [collect(): lax.ppermute(pieces[far - 1], axis, [(d, (d - 1) % ways) for d in range(w...]
    all_gather x3, waiting for transfers between devices: 166 us -> 59 us  [project(): full = lax.all_gather(piece, 'ctx', axis=0, tiled=True)]
    all_gather x1 -> x0, waiting for transfers between devices: 62 us -> none  [body(): lax.all_gather(w_out, 'ctx', axis=0, tiled=True)]
    ppermute x0 -> x7, starting transfers between devices: none -> 37.3 us  [collect(): lax.ppermute(pieces[far - 1], axis, [(d, (d - 1) % ways) for d in range(w...]
    unnamed x13 -> x30, local copies, waits for them, and re-layouts: 9.79 us -> 25.5 us
    ppermute x1, starting transfers between devices: 4.87 us -> 1.29 us  [body(): lax.ppermute(tokens[-2:], 'ctx', perm=[(i, i + 1) for i in range(ctx_coun...]
  transfers between devices with their start and end apart: 5 -> 11, of which waited for: 4 -> 9; matrix products, arithmetic and copies ran while one was open for 9% -> 13% of each run, Pallas kernels for 0% -> 0%
where the time goes in v1:
time: 309 us
  waiting for transfers between devices  170 us (55%)
  blocking collectives  38.8 us (13%)
  starting transfers between devices  38.6 us (12%)
  local copies, waits for them, and re-layouts  30.3 us (10%)
  matrix products  15.8 us (5%)
  between operations  13.3 us (4%)
    ppermute x7, waiting for transfers between devices, collect(): lax.ppermute(pieces[far - 1], axis, [(d, (d - 1) % ways) for d in range(w...  110 us
    all_gather x3, waiting for transfers between devices, project(): full = lax.all_gather(piece, 'ctx', axis=0, tiled=True)  59 us
    ppermute x7, starting transfers between devices, collect(): lax.ppermute(pieces[far - 1], axis, [(d, (d - 1) % ways) for d in range(w...  37.3 us
    all_gather x1, blocking collectives, modal_long_conv(): states = lax.all_gather(end_state, 'ctx', axis=0, tiled=False)  31.8 us
    unnamed x30, local copies, waits for them, and re-layouts  25.5 us
    dot_general x3, matrix products, project(): out = jnp.dot(rows, full, preferred_element_type=jnp.float32)  9.16 us
    all_gather x1, blocking collectives, body(): features = lax.all_gather(gated, 'tp', axis=1, tiled=True)  7.07 us
  transfers between devices with their start and end apart: 11, of which 9 were waited for; matrix products, arithmetic and copies ran while one was open for 13% of the time, Pallas kernels for 0%

profile of v1, /device:TPU:0, one launch (start us, length us, event | category | flops | bytes accessed | tf_op | source)
XLA Modules:
  0.0 308.8 jit_solution(1207877352215855645)
XLA Ops:
  8.1 6.1 %collective-permute-start.1 = (bf16[256,1024]{1,0:T(8,128)(2,1)}, bf16[256,1024]{1,0:T(8,128)(2,1)S(1)}, u32[]{:S(2)}, u32[]{:S(2)}) collective-permute-start(bf16[256,1024]{1,0:T(8,128)(2,1)} %param.21), channel_id=1, source_target_pairs={{0,28},{4,0},{8,4},{12,8},{16,12},{20,16},{24,20},{28,24},{1,29},{... | collective-permute-start | bytes 1572872 | tf_op jit(solution)/shard_map/ppermute | solution.py:12
  14.1 16.9 %collective-permute-done.1 = bf16[256,1024]{1,0:T(8,128)(2,1)S(1)} collective-permute-done((bf16[256,1024]{1,0:T(8,128)(2,1)}, bf16[256,1024]{1,0:T(8,128)(2,1)S(1)}, u32[]{:S(2)}, u32[]{:S(2)}) %collective-permute-start.1) | collective-permute-done | bytes 524320 | tf_op jit(solution)/shard_map/ppermute | solution.py:12
  31.0 5.1 %collective-permute-start.2 = (bf16[256,1024]{1,0:T(8,128)(2,1)S(1)}, bf16[256,1024]{1,0:T(8,128)(2,1)S(1)}, u32[]{:S(2)}, u32[]{:S(2)}) collective-permute-start(bf16[256,1024]{1,0:T(8,128)(2,1)S(1)} %collective-permute-done.1), channel_id=1, source_target_pairs={{0,28},{4,0},{8,4},{12,8},{16,12},{20,16},{24,20},{28,24},{1,29},{... | collective-permute-start | bytes 1572872 | tf_op jit(solution)/shard_map/ppermute | solution.py:12
  36.1 17.4 %collective-permute-done.2 = bf16[256,1024]{1,0:T(8,128)(2,1)S(1)} collective-permute-done((bf16[256,1024]{1,0:T(8,128)(2,1)S(1)}, bf16[256,1024]{1,0:T(8,128)(2,1)S(1)}, u32[]{:S(2)}, u32[]{:S(2)}) %collective-permute-start.2) | collective-permute-done | bytes 524320 | tf_op jit(solution)/shard_map/ppermute | solution.py:12
  53.6 5.2 %collective-permute-start.3 = (bf16[256,1024]{1,0:T(8,128)(2,1)S(1)}, bf16[256,1024]{1,0:T(8,128)(2,1)S(1)}, u32[]{:S(2)}, u32[]{:S(2)}) collective-permute-start(bf16[256,1024]{1,0:T(8,128)(2,1)S(1)} %collective-permute-done.2), channel_id=1, source_target_pairs={{0,28},{4,0},{8,4},{12,8},{16,12},{20,16},{24,20},{28,24},{1,29},{... | collective-permute-start | bytes 1572872 | tf_op jit(solution)/shard_map/ppermute | solution.py:12
  58.8 21.3 %collective-permute-done.3 = bf16[256,1024]{1,0:T(8,128)(2,1)S(1)} collective-permute-done((bf16[256,1024]{1,0:T(8,128)(2,1)S(1)}, bf16[256,1024]{1,0:T(8,128)(2,1)S(1)}, u32[]{:S(2)}, u32[]{:S(2)}) %collective-permute-start.3) | collective-permute-done | bytes 524320 | tf_op jit(solution)/shard_map/ppermute | solution.py:12
  80.1 5.2 %collective-permute-start.4 = (bf16[256,1024]{1,0:T(8,128)(2,1)S(1)}, bf16[256,1024]{1,0:T(8,128)(2,1)S(1)}, u32[]{:S(2)}, u32[]{:S(2)}) collective-permute-start(bf16[256,1024]{1,0:T(8,128)(2,1)S(1)} %collective-permute-done.3), channel_id=1, source_target_pairs={{0,28},{4,0},{8,4},{12,8},{16,12},{20,16},{24,20},{28,24},{1,29},{... | collective-permute-start | bytes 1572872 | tf_op jit(solution)/shard_map/ppermute | solution.py:12
  87.5 19.5 %collective-permute-done.4 = bf16[256,1024]{1,0:T(8,128)(2,1)S(1)} collective-permute-done((bf16[256,1024]{1,0:T(8,128)(2,1)S(1)}, bf16[256,1024]{1,0:T(8,128)(2,1)S(1)}, u32[]{:S(2)}, u32[]{:S(2)}) %collective-permute-start.4) | collective-permute-done | bytes 524320 | tf_op jit(solution)/shard_map/ppermute | solution.py:12
  107.1 5.2 %collective-permute-start.5 = (bf16[256,1024]{1,0:T(8,128)(2,1)S(1)}, bf16[256,1024]{1,0:T(8,128)(2,1)S(1)}, u32[]{:S(2)}, u32[]{:S(2)}) collective-permute-start(bf16[256,1024]{1,0:T(8,128)(2,1)S(1)} %collective-permute-done.4), channel_id=1, source_target_pairs={{0,28},{4,0},{8,4},{12,8},{16,12},{20,16},{24,20},{28,24},{1,29},{... | collective-permute-start | bytes 1572872 | tf_op jit(solution)/shard_map/ppermute | solution.py:12
  113.9 11.1 %collective-permute-done.5 = bf16[256,1024]{1,0:T(8,128)(2,1)S(1)} collective-permute-done((bf16[256,1024]{1,0:T(8,128)(2,1)S(1)}, bf16[256,1024]{1,0:T(8,128)(2,1)S(1)}, u32[]{:S(2)}, u32[]{:S(2)}) %collective-permute-start.5) | collective-permute-done | bytes 524320 | tf_op jit(solution)/shard_map/ppermute | solution.py:12
  125.0 5.2 %collective-permute-start.6 = (bf16[256,1024]{1,0:T(8,128)(2,1)S(1)}, bf16[256,1024]{1,0:T(8,128)(2,1)S(1)}, u32[]{:S(2)}, u32[]{:S(2)}) collective-permute-start(bf16[256,1024]{1,0:T(8,128)(2,1)S(1)} %collective-permute-done.5), channel_id=1, source_target_pairs={{0,28},{4,0},{8,4},{12,8},{16,12},{20,16},{24,20},{28,24},{1,29},{... | collective-permute-start | bytes 1572872 | tf_op jit(solution)/shard_map/ppermute | solution.py:12
  134.6 10.4 %collective-permute-done.6 = bf16[256,1024]{1,0:T(8,128)(2,1)S(1)} collective-permute-done((bf16[256,1024]{1,0:T(8,128)(2,1)S(1)}, bf16[256,1024]{1,0:T(8,128)(2,1)S(1)}, u32[]{:S(2)}, u32[]{:S(2)}) %collective-permute-start.6) | collective-permute-done | bytes 524320 | tf_op jit(solution)/shard_map/ppermute | solution.py:12
  145.0 5.2 %collective-permute-start.7 = (bf16[256,1024]{1,0:T(8,128)(2,1)S(1)}, bf16[256,1024]{1,0:T(8,128)(2,1)S(1)}, u32[]{:S(2)}, u32[]{:S(2)}) collective-permute-start(bf16[256,1024]{1,0:T(8,128)(2,1)S(1)} %collective-permute-done.6), channel_id=1, source_target_pairs={{0,28},{4,0},{8,4},{12,8},{16,12},{20,16},{24,20},{28,24},{1,29},{... | collective-permute-start | bytes 1572872 | tf_op jit(solution)/shard_map/ppermute | solution.py:12
  154.4 12.8 %collective-permute-done.7 = bf16[256,1024]{1,0:T(8,128)(2,1)S(1)} collective-permute-done((bf16[256,1024]{1,0:T(8,128)(2,1)S(1)}, bf16[256,1024]{1,0:T(8,128)(2,1)S(1)}, u32[]{:S(2)}, u32[]{:S(2)}) %collective-permute-start.7) | collective-permute-done | bytes 524320 | tf_op jit(solution)/shard_map/ppermute | solution.py:12
  174.9 3.3 %fusion.14 = f32[130,512]{1,0:T(8,128)S(1)} fusion(bf16[4096,512]{1,0:T(8,128)(2,1)} %all-gather.7.cloned.1.call-done, bf16[128,4096]{1,0:T(8,128)(2,1)} %param.11, bf16[2,4096]{1,0:T(2,128)(2,1)S(1)} %collective-permute-done), kind=kOutput, calls=%fused_computation.15 | convolution fusion | flops 547522560 | bytes 5525504 | tf_op jit(solution)/shard_map/dot_general | solution.py:69
  178.1 34.8 %all-gather.9.cloned.1.call-done = bf16[4096,512]{1,0:T(8,128)(2,1)} async-done(((bf16[512,512]{1,0:T(8,128)(2,1)}), bf16[4096,512]{1,0:T(8,128)(2,1)}) %all-gather.9.cloned.1.call-update) | async-done | bytes 4194320 | tf_op jit(solution)/shard_map/all_gather | solution.py:68
  212.9 2.9 fusion.13
  216.6 3.4 %copy.13 = f32[16,8,16,512]{3,1,2,0:T(8,128)S(1)} copy(f32[16,8,16,512]{3,2,1,0:T(8,128)S(1)} %bitcast.27) | data formatting | bytes 8388608
  220.0 3.0 fusion.4
  225.1 5.6 %copy.14 = f32[16,8,16,512]{3,2,1,0:T(8,128)S(1)} copy(f32[16,8,16,512]{3,1,2,0:T(8,128)} %bitcast.25) | data formatting | bytes 8388608
  230.8 31.8 %all-gather = f32[128,512]{1,0:T(8,128)S(1)} all-gather(f32[16,512]{1,0:T(8,128)S(1)} %get-tuple-element.6), channel_id=2, replica_groups=mesh['ctx'=8,'tp'=4] {'ctx'}, dimensions={0}, use_global_device_ids=true | all-gather | bytes 294912 | tf_op jit(solution)/shard_map/all_gather | solution.py:38
  264.3 24.2 %all-gather.5.cloned.1.call-done = bf16[4096,512]{1,0:T(8,128)(2,1)} async-done(((bf16[512,512]{1,0:T(8,128)(2,1)}), bf16[4096,512]{1,0:T(8,128)(2,1)}) %all-gather.5.cloned.1.call-update) | async-done | bytes 4194320 | tf_op jit(solution)/shard_map/all_gather | solution.py:68
  291.5 7.1 %all_gather.23 = bf16[128,2048]{1,0:T(8,128)(2,1)S(1)} all-gather(bf16[128,512]{1,0:T(8,128)(2,1)S(1)} %multiply_convert_fusion), channel_id=1, replica_groups=mesh['ctx'=8,'tp'=4] {'tp'}, dimensions={1}, use_global_device_ids=true | all-gather | bytes 655360 | tf_op jit(solution)/shard_map/all_gather | solution.py:82
  298.6 3.6 %fusion.10 = bf16[128,1024]{1,0:T(8,128)(2,1)} fusion(bf16[128,2048]{1,0:T(8,128)(2,1)S(1)} %all_gather.23, bf16[4096,1024]{1,0:T(8,128)(2,1)} %constant_dynamic-update-slice_fusion, s32[]{:T(128)S(6)} %select_n.19), kind=kOutput, calls=%fused_computation.11 | convolution fusion | flops 537001984 | bytes 4980740 | tf_op jit(solution)/shard_map/dot_general | solution.py:83
  (54 shorter events, 28.9 us)
Async XLA Ops:
  6.5 168.3 %all-gather.7.cloned.1.call-start = ((), (), s32[]{:S(2)}) async-start(), calls=%async_computation.1 | async-start | bytes 4718592 | tf_op jit(solution)/shard_map/all_gather | solution.py:68
  7.3 205.7 %all-gather.9.cloned.1.call-start = ((), (), s32[]{:S(2)}) async-start(), calls=%async_computation.2 | async-start | bytes 4718592 | tf_op jit(solution)/shard_map/all_gather | solution.py:68
  8.0 280.4 %all-gather.5.cloned.1.call-start = ((), (), s32[]{:S(2)}) async-start(), calls=%async_computation | async-start | bytes 4718592 | tf_op jit(solution)/shard_map/all_gather | solution.py:68
  8.1 23.0 %collective-permute-start.1 = (bf16[256,1024]{1,0:T(8,128)(2,1)}, bf16[256,1024]{1,0:T(8,128)(2,1)S(1)}, u32[]{:S(2)}, u32[]{:S(2)}) collective-permute-start(bf16[256,1024]{1,0:T(8,128)(2,1)} %param.21), channel_id=1, source_target_pairs={{0,28},{4,0},{8,4},{12,8},{16,12},{20,16},{24,20},{28,24},{1,29},{... | collective-permute-start | bytes 1572872 | tf_op jit(solution)/shard_map/ppermute | solution.py:12
  31.0 22.6 %collective-permute-start.2 = (bf16[256,1024]{1,0:T(8,128)(2,1)S(1)}, bf16[256,1024]{1,0:T(8,128)(2,1)S(1)}, u32[]{:S(2)}, u32[]{:S(2)}) collective-permute-start(bf16[256,1024]{1,0:T(8,128)(2,1)S(1)} %collective-permute-done.1), channel_id=1, source_target_pairs={{0,28},{4,0},{8,4},{12,8},{16,12},{20,16},{24,20},{28,24},{1,29},{... | collective-permute-start | bytes 1572872 | tf_op jit(solution)/shard_map/ppermute | solution.py:12
  53.6 26.5 %collective-permute-start.3 = (bf16[256,1024]{1,0:T(8,128)(2,1)S(1)}, bf16[256,1024]{1,0:T(8,128)(2,1)S(1)}, u32[]{:S(2)}, u32[]{:S(2)}) collective-permute-start(bf16[256,1024]{1,0:T(8,128)(2,1)S(1)} %collective-permute-done.2), channel_id=1, source_target_pairs={{0,28},{4,0},{8,4},{12,8},{16,12},{20,16},{24,20},{28,24},{1,29},{... | collective-permute-start | bytes 1572872 | tf_op jit(solution)/shard_map/ppermute | solution.py:12
  80.1 26.9 %collective-permute-start.4 = (bf16[256,1024]{1,0:T(8,128)(2,1)S(1)}, bf16[256,1024]{1,0:T(8,128)(2,1)S(1)}, u32[]{:S(2)}, u32[]{:S(2)}) collective-permute-start(bf16[256,1024]{1,0:T(8,128)(2,1)S(1)} %collective-permute-done.3), channel_id=1, source_target_pairs={{0,28},{4,0},{8,4},{12,8},{16,12},{20,16},{24,20},{28,24},{1,29},{... | collective-permute-start | bytes 1572872 | tf_op jit(solution)/shard_map/ppermute | solution.py:12
  86.2 88.6 %collective-permute-start = (bf16[2,4096]{1,0:T(2,128)(2,1)S(1)}, bf16[2,4096]{1,0:T(2,128)(2,1)S(1)}, u32[]{:S(2)}, u32[]{:S(2)}) collective-permute-start(bf16[2,4096]{1,0:T(2,128)(2,1)S(1)} %slice.62), channel_id=1, source_target_pairs={{0,4},{4,8},{8,12},{12,16},{16,20},{20,24},{24,28},{1,5},{5,9},{9,... | collective-permute-start | bytes 49160 | tf_op jit(solution)/shard_map/ppermute | solution.py:64
  107.1 17.9 %collective-permute-start.5 = (bf16[256,1024]{1,0:T(8,128)(2,1)S(1)}, bf16[256,1024]{1,0:T(8,128)(2,1)S(1)}, u32[]{:S(2)}, u32[]{:S(2)}) collective-permute-start(bf16[256,1024]{1,0:T(8,128)(2,1)S(1)} %collective-permute-done.4), channel_id=1, source_target_pairs={{0,28},{4,0},{8,4},{12,8},{16,12},{20,16},{24,20},{28,24},{1,29},{... | collective-permute-start | bytes 1572872 | tf_op jit(solution)/shard_map/ppermute | solution.py:12
  125.0 20.0 %collective-permute-start.6 = (bf16[256,1024]{1,0:T(8,128)(2,1)S(1)}, bf16[256,1024]{1,0:T(8,128)(2,1)S(1)}, u32[]{:S(2)}, u32[]{:S(2)}) collective-permute-start(bf16[256,1024]{1,0:T(8,128)(2,1)S(1)} %collective-permute-done.5), channel_id=1, source_target_pairs={{0,28},{4,0},{8,4},{12,8},{16,12},{20,16},{24,20},{28,24},{1,29},{... | collective-permute-start | bytes 1572872 | tf_op jit(solution)/shard_map/ppermute | solution.py:12
  131.0 37.1 %copy-start.1 = (bf16[256,1024]{1,0:T(8,128)(2,1)S(1)}, bf16[256,1024]{1,0:T(8,128)(2,1)}, u32[]{:S(2)}) copy-start(bf16[256,1024]{1,0:T(8,128)(2,1)} %param.21) | copy-start | bytes 1572868
  145.0 22.2 %collective-permute-start.7 = (bf16[256,1024]{1,0:T(8,128)(2,1)S(1)}, bf16[256,1024]{1,0:T(8,128)(2,1)S(1)}, u32[]{:S(2)}, u32[]{:S(2)}) collective-permute-start(bf16[256,1024]{1,0:T(8,128)(2,1)S(1)} %collective-permute-done.6), channel_id=1, source_target_pairs={{0,28},{4,0},{8,4},{12,8},{16,12},{20,16},{24,20},{28,24},{1,29},{... | collective-permute-start | bytes 1572872 | tf_op jit(solution)/shard_map/ppermute | solution.py:12
  173.1 39.8 %copy-start.5 = (bf16[128,4096]{1,0:T(8,128)(2,1)S(1)}, bf16[128,4096]{1,0:T(8,128)(2,1)}, u32[]{:S(2)}) copy-start(bf16[128,4096]{1,0:T(8,128)(2,1)} %param.11) | copy-start | bytes 3145732
  223.1 1.9 copy-start
  225.1 5.7 %copy-start.2 = (f32[16,512]{1,0:T(8,128)S(1)}, f32[16,512]{1,0:T(8,128)}, u32[]{:S(2)}) copy-start(f32[16,512]{1,0:T(8,128)} %param.18) | copy-start | bytes 98308
  225.1 5.7 %copy-start.3 = (f32[16,512]{1,0:T(8,128)S(1)}, f32[16,512]{1,0:T(8,128)}, u32[]{:S(2)}) copy-start(f32[16,512]{1,0:T(8,128)} %param.19) | copy-start | bytes 98308
  262.7 28.7 %copy-start.4 = (f32[512]{0:T(512)S(1)}, f32[512]{0:T(512)}, u32[]{:S(2)}) copy-start(f32[512]{0:T(512)} %param.20) | copy-start | bytes 6148
Sparse Core Ops, SparseCore 0:
  9.5 109.7 all-gather.6
  121.4 91.4 all-gather.8
  215.1 73.3 all-gather.4
